TPU v7x, 256 devices: a whole 4x4x8 slice. The times are simulated.
256 devices in a mesh: blk: 64 (over y, z, core), lev: 4 (over x).
Axes of the slice: x: 4, y: 4, z: 8, core: 2. Of those that a mesh axis runs over, the one named last changes fastest.
Arguments:
- adjoint_in: float32 [4096, 12, 1024], P('blk', 'lev'), may hold values from -6 to 6
- courant: float32 [2, 4096, 12, 1024], P(None, 'blk', 'lev'), may hold values from 0.05 to 0.45
- mixing: float32 [4096, 12, 1024], P('blk', 'lev'), may hold values from 0.5 to 8
- oh_rate: float32 [4096, 12, 1024], P('blk', 'lev'), may hold values from 0.02 to 0.6
- substeps: int32 [4096], P('blk'), may hold values from 1 to 4
- nest_weight: float32 [4096, 128], P('blk'), may hold values from 0.2 to 0.9
- dest_device: int32 [4096, 1], P('blk'), may hold values from 0 to 63; in each aligned block of 64 rows (0 to 63, 64 to 127, ...) at most 2 rows name the same one
- dest_slot: int32 [4096], P('blk'), may hold values from 0 to 63
- emission_profile: float32 [12], P('lev'), may hold values from 0.05 to 1
- tile_owner: int32 [4096], P('blk'), may hold values from 0 to 1023, as said below
Outputs:
- adjoint_out: float32 [4096, 12, 1024], P('blk', 'lev')
- tile_grad: float32 [1024, 1024], P(('blk', 'lev'))
Inputs may be any that keep to these rules, and one draw needn't show every extreme that they name: Of the 64 blocks of one index of blk, at most 2 have the same dest_device. Tiles form 64 groups of 16 consecutive tiles. Of the 64 blocks of one index of blk, at most 2 have tile_owner in the same group, and some group holds exactly 2 of them.
All inputs are finite; a program needn't handle non-finite values.
Results may differ from a plain program's by a relative error of at most 0.0003.
Values sent between devices are 32-bit elements; how exact they have to be, the bound alone decides.
No kernel may reach another device: no remote copies, remote signals or barrier semaphores. Data moves between devices by JAX's collectives and lax.ppermute only.
A program may use at most 128 MiB of HBM per device.

v0:
```python
import jax
import jax.numpy as jnp
from jax import lax
from jax.sharding import PartitionSpec as P

RMAX = 4
STEPS = 2


def solve_columns(right_side, coupling):
    level_count = right_side.shape[1]
    ratios = []
    scaled = []
    for level in range(level_count):
        lower_k = coupling[:, level - 1] if level > 0 else 0.0
        upper_k = coupling[:, level] if level < level_count - 1 else 0.0
        diag_term = 1.0 + lower_k + upper_k
        if level == 0:
            pivot_val = diag_term
            scaled.append(right_side[:, 0] / pivot_val)
        else:
            pivot_val = diag_term + lower_k * ratios[level - 1]
            scaled.append((right_side[:, level] + lower_k * scaled[level - 1]) / pivot_val)
        ratios.append(-upper_k / pivot_val)
    solved = [None] * level_count
    solved[level_count - 1] = scaled[level_count - 1]
    for level in range(level_count - 2, -1, -1):
        solved[level] = scaled[level] - ratios[level] * solved[level + 1]
    return jnp.stack(solved, axis=1)


def stencil(adjoint, east_u, north_u, side_len):
    shape_grid = adjoint.shape[:-1] + (side_len, side_len)
    grid_view = adjoint.reshape(shape_grid)
    east_c = east_u.reshape(shape_grid)
    north_c = north_u.reshape(shape_grid)
    zero_col = jnp.zeros(shape_grid[:-1] + (1,), jnp.float32)
    east_adj = jnp.concatenate([grid_view[..., 1:], zero_col], axis=-1)
    zero_row = jnp.zeros(shape_grid[:-2] + (1, side_len), jnp.float32)
    north_adj = jnp.concatenate([grid_view[..., 1:, :], zero_row], axis=-2)
    result = (1.0 - east_c - north_c) * grid_view + east_c * east_adj + north_c * north_adj
    return result.reshape(adjoint.shape)


def faces(adjoint, side_len):
    grid_view = adjoint.reshape(adjoint.shape[:-1] + (side_len, side_len))
    return jnp.concatenate(
        [
            grid_view[..., 0, :],
            grid_view[..., side_len - 1, :],
            grid_view[..., :, 0],
            grid_view[..., :, side_len - 1],
        ],
        axis=-1,
    )


def add_faces(adjoint, arrivals, side_len):
    grid_view = adjoint.reshape(adjoint.shape[:-1] + (side_len, side_len))
    grid_view = grid_view.at[..., 0, :].add(arrivals[..., 0:side_len])
    grid_view = grid_view.at[..., side_len - 1, :].add(arrivals[..., side_len : 2 * side_len])
    grid_view = grid_view.at[..., :, 0].add(arrivals[..., 2 * side_len : 3 * side_len])
    grid_view = grid_view.at[..., :, side_len - 1].add(arrivals[..., 3 * side_len :])
    return grid_view.reshape(adjoint.shape)


def route_cycles(cycle_flat, key_float, own_keys):
    all_cycles, all_keys = (
        lax.all_gather(cycle_flat, "blk", axis=0, tiled=True),
        lax.all_gather(key_float[:, None], "blk", axis=0, tiled=True),
    )
    picking = (all_keys[:, 0][None, :] == own_keys[:, None]).astype(jnp.float32)
    return jnp.dot(picking, all_cycles, precision=lax.Precision.HIGHEST)


def local(
    adjoint_in,
    courant,
    mixing,
    oh_rate,
    substeps,
    nest_weight,
    dest_device,
    dest_slot,
    emission_profile,
    tile_owner,
):
    blocks, lev_dev, cell_count = adjoint_in.shape
    cycle_len = nest_weight.shape[1]
    side_len = cycle_len // 4
    peer_count = lax.axis_size("blk")
    lev_groups = lax.axis_size("lev")
    my_block = lax.axis_index("blk")
    survive = jnp.exp(-oh_rate)
    dest_index = dest_device[:, 0]
    key_float = (dest_index * blocks + dest_slot + 1).astype(jnp.float32)
    own_keys = (my_block * blocks + jnp.arange(blocks, dtype=jnp.int32) + 1).astype(jnp.float32)
    column_mixing = lax.all_to_all(mixing, "lev", split_axis=2, concat_axis=1, tiled=True)
    adjoint = adjoint_in
    grad_sum = jnp.zeros((blocks, cell_count), jnp.float32)
    for step_index in range(STEPS):
        grad_sum = grad_sum + jnp.sum(adjoint * emission_profile[None, :, None], axis=1)
        columns = lax.all_to_all(adjoint * survive, "lev", split_axis=2, concat_axis=1, tiled=True)
        solved = solve_columns(columns, column_mixing)
        adjoint = lax.all_to_all(solved, "lev", split_axis=1, concat_axis=2, tiled=True)
        cycle_out = faces(adjoint, side_len) * nest_weight[:, None, :]
        arrivals = route_cycles(cycle_out.reshape(blocks, -1), key_float, own_keys)
        arrivals = arrivals.reshape(cycle_out.shape)
        advected = adjoint
        for substep in range(RMAX):
            active = (substep < substeps)[:, None, None]
            advected = jnp.where(
                active, stencil(advected, courant[0], courant[1], side_len), advected
            )
        adjoint = add_faces(advected, arrivals, side_len)
    tiles_total = blocks * peer_count // 4
    tile_rows = jnp.arange(
        lax.axis_size(("blk", "lev")) * (tiles_total // (peer_count * lev_groups)), dtype=jnp.int32
    )
    tile_hot = (tile_owner[None, :] == tile_rows[:, None]).astype(jnp.float32)
    tile_grad = lax.psum_scatter(
        jnp.dot(tile_hot, grad_sum, precision=lax.Precision.HIGHEST),
        ("blk", "lev"),
        scatter_dimension=0,
        tiled=True,
    )
    return (adjoint, tile_grad)


def solution(mesh):
    placed = (
        P("blk", "lev", None),
        P(None, "blk", "lev", None),
        P("blk", "lev", None),
        P("blk", "lev", None),
        P("blk"),
        P("blk", None),
        P("blk", None),
        P("blk"),
        P("lev"),
        P("blk"),
    )
    return jax.shard_map(
        local,
        mesh=mesh,
        in_specs=placed,
        out_specs=(P("blk", "lev", None), P(("blk", "lev"), None)),
        check_vma=False,
    )
```

profile of v0, /device:TPU:1, one launch (start us, length us, event | category | flops | bytes accessed | tf_op | source)
XLA Modules:
  0.0 777.3 jit_solution(1277644381630115909)
XLA Ops:
  11.6 5.0 all-to-all-start.1
  22.7 4.0 all-to-all-done.1
  26.8 4.2 all-to-all-start
  31.5 2.9 reduce.17
  36.3 3.8 all-to-all-done
  40.2 4.7 reduce.18
  61.2 3.5 all-to-all-start.2
  64.9 8.1 %all-to-all-done.2 = f32[64,12,256]{2,0,1:T(8,128)S(1)} async-done(((f32[64,12,256]{2,0,1:T(8,128)}), f32[64,12,256]{2,0,1:T(8,128)S(1)}, u32[]{:S(2)}, u32[]{:S(2)}) %all-to-all-start.2) | async-done | bytes 786464 | tf_op jit(solution)/shard_map/all_to_all | solution.py:105
  80.6 264.6 %all-reduce.16 = f32[4096]{0:T(1024)S(1)} all-reduce(f32[4096]{0:T(1024)S(1)} %fusion.43), channel_id=2, replica_groups=mesh['blk'=64,'lev'=4] {'blk'}, use_global_device_ids=true, to_apply=%add.16 | all-reduce | flops 4096 | bytes 32768
  353.7 5.8 fusion.2
  370.6 2.7 scatter-add.30
  374.4 2.8 scatter-add.31
  377.1 2.7 copy.173
  382.3 2.7 copy.174
  384.9 4.3 reshape.377
  389.2 4.2 all-to-all-start.3
  398.0 4.9 fusion.10
  403.0 4.7 reduce.19
  407.7 3.7 reshape.378
  418.7 13.0 %all_to_all.84 = f32[64,12,256]{2,0,1:T(8,128)} all-to-all(f32[64,12,256]{2,0,1:T(8,128)S(1)} %constant_dynamic-update-slice_fusion.11), channel_id=1, replica_groups=mesh['blk'=64,'lev'=4] {'lev'}, dimensions={1} | all-to-all | bytes 1572864 | tf_op jit(solution)/shard_map/all_to_all | solution.py:105
  431.8 2.8 copy.177
  447.7 223.3 %all-reduce.20.cloned.1.call-done = f32[1024,1024]{1,0:T(8,128)} async-done(((f32[1024,1024]{1,0:T(8,128)}), f32[1024,1024]{1,0:T(8,128)}) %all-reduce.20.cloned.1.call-update) | async-done | bytes 4194320
  672.4 83.4 %all-gather.6.cloned.1.call-done = f32[4096,384]{1,0:T(8,128)} async-done(((f32[64,384]{1,0:T(8,128)}), f32[4096,384]{1,0:T(8,128)}) %all-gather.6.cloned.1.call-update) | async-done | bytes 6291472 | tf_op jit(solution)/shard_map/all_gather | solution.py:69
  755.8 7.8 %fusion = f32[64,384]{0,1:T(8,128)S(1)} fusion(f32[4096,384]{1,0:T(8,128)} %all-gather.6.cloned.1.call-done, f32[4096]{0:T(1024)S(1)} %all-reduce.16, f32[64]{0:T(128)S(1)} %copy-done.33), kind=kOutput, calls=%fused_computation.10 | convolution fusion | flops 1208221696 | bytes 6406400 | tf_op jit(solution)/shard_map/reshape | solution.py:108
  (191 shorter events, 92.0 us)
Async XLA Ops:
  9.0 7.5 copy-start.34
  11.6 5.0 copy-start.6
  11.6 5.0 copy-start.19
  11.6 15.2 %all-to-all-start.1 = ((f32[4,1,49152]{2,1,0:T(1,128)}), f32[4,1,49152]{2,1,0:T(1,128)S(1)}, u32[]{:S(2)}, u32[]{:S(2)}) async-start(f32[4,1,49152]{2,1,0:T(1,128)} %reshape.373), calls=%async_computation.1 | async-start | bytes 1572864 | tf_op jit(solution)/shard_map/all_to_all | solution.py:98
  26.8 13.4 %all-to-all-start = ((f32[4,1,49152]{2,1,0:T(1,128)}), f32[4,1,49152]{2,1,0:T(1,128)}, u32[]{:S(2)}, u32[]{:S(2)}) async-start(f32[4,1,49152]{2,1,0:T(1,128)} %reshape.375), calls=%async_computation | async-start | bytes 1572864 | tf_op jit(solution)/shard_map/all_to_all | solution.py:103
  36.3 23.4 %copy-start.3 = (f32[64,4,3,256]{3,0,2,1:T(8,128)}, f32[64,4,3,256]{3,0,2,1:T(8,128)S(1)}, u32[]{:S(2)}) copy-start(f32[64,4,3,256]{3,0,2,1:T(8,128)S(1)} %copy.164) | copy-start | bytes 2359300
  50.6 4.4 copy-start.7
  50.6 4.4 copy-start.9
  55.0 9.7 %copy-start.23 = (f32[64,128]{1,0:T(8,128)S(1)}, f32[64,128]{1,0:T(8,128)}, u32[]{:S(2)}) copy-start(f32[64,128]{1,0:T(8,128)} %param.31) | copy-start | bytes 98308
  61.2 11.8 %all-to-all-start.2 = ((f32[64,12,256]{2,0,1:T(8,128)}), f32[64,12,256]{2,0,1:T(8,128)S(1)}, u32[]{:S(2)}, u32[]{:S(2)}) async-start(f32[64,12,256]{2,0,1:T(8,128)} %constant_dynamic-update-slice_fusion), calls=%async_computation.2 | async-start | bytes 1572864 | tf_op jit(solution)/shard_map/all_to_all | solution.py:105
  64.7 288.9 %all-gather.4.cloned.1.call-start = ((), (), s32[]{:S(2)}) async-start(), calls=%async_computation.5 | async-start | bytes 6389760 | tf_op jit(solution)/shard_map/all_gather | solution.py:69
  64.9 8.8 %copy-start.20 = (f32[64,128]{0,1:T(8,128)}, f32[64,128]{0,1:T(8,128)S(1)}, u32[]{:S(2)}) copy-start(f32[64,128]{0,1:T(8,128)S(1)} %copy.167) | copy-start | bytes 98308
  77.7 267.5 %copy-start.37 = (s32[64]{0:T(128)S(1)}, s32[64]{0:T(128)}, u32[]{:S(2)}) copy-start(s32[64]{0:T(128)} %param.30) | copy-start | bytes 772
  345.2 8.5 %copy-start.32 = (f32[64]{0:T(128)}, f32[64]{0:T(128)S(1)}, u32[]{:S(2)}) copy-start(f32[64]{0:T(128)S(1)} %add_convert_fusion) | copy-start | bytes 772
  345.2 4.9 copy-start.26
  345.2 6.3 copy-start.24
  384.9 8.6 %copy-start.35 = (f32[3]{0:T(128)S(1)}, f32[3]{0:T(128)}, u32[]{:S(2)}) copy-start(f32[3]{0:T(128)} %param.34) | copy-start | bytes 40
  389.2 13.7 %all-to-all-start.3 = ((f32[4,1,49152]{2,1,0:T(1,128)}), f32[4,1,49152]{2,1,0:T(1,128)}, u32[]{:S(2)}, u32[]{:S(2)}) async-start(f32[4,1,49152]{2,1,0:T(1,128)} %reshape.377), calls=%async_computation.3 | async-start | bytes 1572864 | tf_op jit(solution)/shard_map/all_to_all | solution.py:103
  393.5 4.5 copy-start.36
  393.5 277.5 %all-reduce.20.cloned.1.call-start = ((), (), s32[]{:S(2)}) async-start(), calls=%async_computation.7 | async-start | bytes 8388608
  402.9 352.8 %all-gather.6.cloned.1.call-start = ((), (), s32[]{:S(2)}) async-start(), calls=%async_computation.6 | async-start | bytes 6389760 | tf_op jit(solution)/shard_map/all_gather | solution.py:69
  431.8 4.8 copy-start.21
  445.5 310.2 %copy-start.33 = (f32[64]{0:T(128)S(1)}, f32[64]{0:T(128)}, u32[]{:S(2)}) copy-start(f32[64]{0:T(128)} %copy-done.32) | copy-start | bytes 772
  672.3 91.3 %copy-start.5 = (f32[64,3,32,32]{0,3,2,1:T(8,128)S(1)}, f32[64,3,32,32]{0,3,2,1:T(8,128)}, u32[]{:S(2)}) copy-start(f32[64,3,32,32]{0,3,2,1:T(8,128)} %add_select_fusion) | copy-start | bytes 2359300
  (24 other events, 55.2 us)
Sparse Core Ops, SparseCore 0:
  74.8 88.7 all-gather.3
  403.1 267.8 all-reduce.19
  674.3 81.4 all-gather.5
where the time goes:
time: 788 us; the launch traced here: 777 us
  waiting for transfers between devices  323 us (41%)
  blocking collectives  278 us (35%)
  local copies, waits for them, and re-layouts  77.4 us (10%)
  other arithmetic  48.5 us (6%)
  matrix products  18.5 us (2%)
  starting transfers between devices  17 us (2%)
  between operations  15.5 us (2%)
    unnamed x1, blocking collectives  265 us
    unnamed x4, waiting for transfers between devices  223 us
    all_gather x2, waiting for transfers between devices, route_cycles(): lax.all_gather(cycle_flat, 'blk', axis=0, tiled=True)  83.4 us
    unnamed x108, local copies, waits for them, and re-layouts  31.9 us
  transfers between devices with their start and end apart: 7, of which 5 were waited for; matrix products, arithmetic and copies ran while one was open for 8% of the time, Pallas kernels for 0%

commit v1 on v0

--- a/solution.py
+++ b/solution.py
@@ -1,3 +1,4 @@
+import functools
 import jax
 import jax.numpy as jnp
 from jax import lax
@@ -5,6 +6,19 @@
 
 RMAX = 4
 STEPS = 2
+
+
+def process_the_rails(s0, axis_id):
+    right_arr = jnp.concatenate(
+        lax.all_to_all(
+            jnp.stack([s0] * lax.axis_size(axis_id)), axis_name=axis_id, split_axis=0, concat_axis=0
+        ),
+        axis=0,
+    )
+    return right_arr
+
+
+see_space = functools.partial(process_the_rails, axis_id="blk")
 
 
 def solve_columns(right_side, coupling):
@@ -66,7 +80,7 @@
 
 def route_cycles(cycle_flat, key_float, own_keys):
     all_cycles, all_keys = (
-        lax.all_gather(cycle_flat, "blk", axis=0, tiled=True),
+        see_space(cycle_flat),
         lax.all_gather(key_float[:, None], "blk", axis=0, tiled=True),
     )
     picking = (all_keys[:, 0][None, :] == own_keys[:, None]).astype(jnp.float32)

time: 788 us -> 1040 us (1.32)
  local copies, waits for them, and re-layouts: 77.4 us -> 184 us
  blocking collectives: 278 us -> 383 us
  other arithmetic: 48.5 us -> 79.6 us
  starting transfers between devices: 17 us -> 46.8 us
  waiting for transfers between devices: 323 us -> 300 us
    unnamed x1, blocking collectives: 265 us -> 358 us
    all_gather x2 -> x0, waiting for transfers between devices: 83.4 us -> none  [route_cycles(): lax.all_gather(cycle_flat, 'blk', axis=0, tiled=True)]
    unnamed x4 -> x2, waiting for transfers between devices: 223 us -> 285 us
    scatter-add x2 -> x4, local copies, waits for them, and re-layouts: 5.34 us -> 58.1 us  [the longest x2 34.9 us: add_faces(): grid_view.at[..., side_len - 1, :].add(arrivals[..., side_len:2 * side_len])]
    all_to_all x0 -> x2, starting transfers between devices: none -> 34.3 us  [process_the_rails(): lax.all_to_all(jnp.stack([s0] * lax.axis_size(axis_id)), axis_name=axis_i...]
    another operation x0 -> x10, local copies, waits for them, and re-layouts: none -> 29.2 us
    add x4, other arithmetic: 2.27 us -> 19.8 us  [the longest x2 9.93 us: add_faces(): grid_view = grid_view.at[..., 0, :].add(arrivals[..., 0:side_len])]
    dot_general x0 -> x2, local copies, waits for them, and re-layouts: none -> 13.2 us  [route_cycles(): return jnp.dot(picking, all_cycles, precision=lax.Precision.HIGHEST)]
  transfers between devices with their start and end apart: 7 -> 6, of which waited for: 5 -> 4; matrix products, arithmetic and copies ran while one was open for 8% -> 8% of each run, Pallas kernels for 0% -> 0%
where the time goes in v1:
time: 1040 us; the launch traced here: 1030 us
  blocking collectives  383 us (37%)
  waiting for transfers between devices  300 us (29%)
  local copies, waits for them, and re-layouts  184 us (18%)
  other arithmetic  79.6 us (8%)
  starting transfers between devices  46.8 us (4%)
  matrix products  17.1 us (2%)
  between operations  15.6 us (2%)
    unnamed x1, blocking collectives  358 us
    unnamed x2, waiting for transfers between devices  285 us
    scatter-add x2, local copies, waits for them, and re-layouts, add_faces(): grid_view.at[..., side_len - 1, :].add(arrivals[..., side_len:2 * side_len])  34.9 us
    all_to_all x2, starting transfers between devices, process_the_rails(): lax.all_to_all(jnp.stack([s0] * lax.axis_size(axis_id)), axis_name=axis_i...  34.3 us
    unnamed x70, local copies, waits for them, and re-layouts  33.4 us
    scatter-add x2, local copies, waits for them, and re-layouts, add_faces(): grid_view = grid_view.at[..., 0, :].add(arrivals[..., 0:side_len])  23.3 us
  transfers between devices with their start and end apart: 6, of which 4 were waited for; matrix products, arithmetic and copies ran while one was open for 8% of the time, Pallas kernels for 0%

profile of v1, /device:TPU:1, one launch (start us, length us, event | category | flops | bytes accessed | tf_op | source)
XLA Modules:
  0.0 1026.0 jit_solution(12724613031366319189)
XLA Ops:
  11.6 4.8 all-to-all-start.1
  40.0 4.8 reduce.18
  64.7 8.2 all-to-all-done.2
  77.0 21.2 %all-to-all-start.3 = ((f32[64,64,384]{2,1,0:T(8,128)}), f32[64,64,384]{2,1,0:T(8,128)}, u32[]{:S(2)}, u32[]{:S(2)}) async-start(f32[64,64,384]{2,1,0:T(8,128)} %stack.9), calls=%async_computation.3 | async-start | bytes 12582912 | tf_op jit(solution)/shard_map/all_to_all | solution.py:13
  110.7 358.2 %all-reduce.16 = f32[4096]{0:T(1024)S(1)} all-reduce(f32[4096]{0:T(1024)S(1)} %fusion.47), channel_id=2, replica_groups=mesh['blk'=64,'lev'=4] {'blk'}, use_global_device_ids=true, to_apply=%add.16 | all-reduce | flops 4096 | bytes 32768
  491.0 6.6 copy.283
  497.6 6.2 fusion.2
  508.9 4.4 copy.287
  513.3 5.4 slice_add_fusion.3
  518.8 8.3 scatter-add.26
  527.1 5.4 slice_add_fusion.2
  532.5 12.5 %scatter-add.29 = f32[64,3,32,32]{2,0,1,3:T(8,128)} dynamic-update-slice(f32[64,3,32,32]{2,0,1,3:T(8,128)} %scatter-add.26, f32[64,3,1,32]{2,0,1,3:T(8,128)} %slice_add_fusion.2, s32[]{:T(128)} %constant.203.clone.1, s32[]{:T(128)} %constant.203.clone.1, s32[]{:T(128)} %constant.208.clone.1, s32[]{:T(128)} %constant.203.clone.1) | dynamic-update-slice | bytes 49156 | tf_op jit(solution)/shard_map/scatter-add | solution.py:75
  563.7 13.0 %all_to_all.94 = f32[4,1,49152]{2,1,0:T(1,128)} all-to-all(f32[4,1,49152]{2,1,0:T(1,128)} %reshape.386), channel_id=1, replica_groups=mesh['blk'=64,'lev'=4] {'lev'}, dimensions={0} | all-to-all | bytes 1572864 | tf_op jit(solution)/shard_map/all_to_all | solution.py:117
  576.7 4.7 reduce.19
  592.7 11.5 %all_to_all.95 = f32[64,12,256]{2,0,1:T(8,128)} all-to-all(f32[64,12,256]{2,0,1:T(8,128)S(1)} %constant_dynamic-update-slice_fusion.11), channel_id=1, replica_groups=mesh['blk'=64,'lev'=4] {'lev'}, dimensions={1} | all-to-all | bytes 1572864 | tf_op jit(solution)/shard_map/all_to_all | solution.py:119
  613.3 13.0 %all-to-all-start.6 = ((f32[64,64,384]{2,1,0:T(8,128)}), f32[64,64,384]{2,1,0:T(8,128)}, u32[]{:S(2)}, u32[]{:S(2)}) async-start(f32[64,64,384]{2,1,0:T(8,128)} %stack.11), calls=%async_computation.6 | async-start | bytes 12582912 | tf_op jit(solution)/shard_map/all_to_all | solution.py:13
  633.6 4.7 fusion.12
  660.5 285.4 %all-reduce.20.cloned.1.call-done = f32[1024,1024]{1,0:T(8,128)} async-done(((f32[1024,1024]{1,0:T(8,128)}), f32[1024,1024]{1,0:T(8,128)}) %all-reduce.20.cloned.1.call-update) | async-done | bytes 4194320
  947.3 6.6 copy.311
  953.9 6.2 fusion
  963.8 4.5 slice_add_fusion.1
  968.3 14.9 %scatter-add.34 = f32[64,3,32,32]{2,0,1,3:T(8,128)S(1)} dynamic-update-slice(f32[64,3,32,32]{2,0,1,3:T(8,128)S(1)} %copy-done.2, f32[64,3,1,32]{2,0,1,3:T(8,128)} %slice_add_fusion.1, s32[]{:T(128)} %constant.203.clone.1, s32[]{:T(128)} %constant.203.clone.1, s32[]{:T(128)} %constant.203.clone.1, s32[]{:T(128)} %constant.203.clone.1) | dynamic-update-slice | bytes 49156 | tf_op jit(solution)/shard_map/scatter-add | solution.py:74
  986.9 4.4 slice_add_fusion
  991.3 22.4 %scatter-add.35 = f32[64,3,32,32]{2,0,1,3:T(8,128)S(1)} dynamic-update-slice(f32[64,3,32,32]{2,0,1,3:T(8,128)S(1)} %scatter-add.34, f32[64,3,1,32]{2,0,1,3:T(8,128)} %slice_add_fusion, s32[]{:T(128)} %constant.203.clone.1, s32[]{:T(128)} %constant.203.clone.1, s32[]{:T(128)} %constant.208.clone.1, s32[]{:T(128)} %constant.203.clone.1) | dynamic-update-slice | bytes 49156 | tf_op jit(solution)/shard_map/scatter-add | solution.py:75
  (164 shorter events, 172.8 us)
Async XLA Ops:
  7.2 9.2 copy-start.17
  11.6 15.1 %all-to-all-start.1 = ((f32[4,1,49152]{2,1,0:T(1,128)}), f32[4,1,49152]{2,1,0:T(1,128)S(1)}, u32[]{:S(2)}, u32[]{:S(2)}) async-start(f32[4,1,49152]{2,1,0:T(1,128)} %reshape.382), calls=%async_computation.1 | async-start | bytes 1572864 | tf_op jit(solution)/shard_map/all_to_all | solution.py:112
  26.6 13.4 %all-to-all-start = ((f32[4,1,49152]{2,1,0:T(1,128)}), f32[4,1,49152]{2,1,0:T(1,128)}, u32[]{:S(2)}, u32[]{:S(2)}) async-start(f32[4,1,49152]{2,1,0:T(1,128)} %reshape.384), calls=%async_computation | async-start | bytes 1572864 | tf_op jit(solution)/shard_map/all_to_all | solution.py:117
  36.2 23.4 %copy-start.5 = (f32[64,4,3,256]{3,0,2,1:T(8,128)}, f32[64,4,3,256]{3,0,2,1:T(8,128)S(1)}, u32[]{:S(2)}) copy-start(f32[64,4,3,256]{3,0,2,1:T(8,128)S(1)} %copy.266) | copy-start | bytes 2359300
  50.5 10.5 %copy-start.7 = (f32[64,1,256]{2,0,1:T(8,128)}, f32[64,1,256]{2,0,1:T(8,128)S(1)}, u32[]{:S(2)}) copy-start(f32[64,1,256]{2,0,1:T(8,128)S(1)} %get-tuple-element.150) | copy-start | bytes 196612
  50.5 10.5 %copy-start.10 = (f32[64,1,256]{2,0,1:T(8,128)}, f32[64,1,256]{2,0,1:T(8,128)S(1)}, u32[]{:S(2)}) copy-start(f32[64,1,256]{2,0,1:T(8,128)S(1)} %get-tuple-element.134) | copy-start | bytes 196612
  50.5 10.5 %copy-start.11 = (f32[64,1,256]{2,0,1:T(8,128)}, f32[64,1,256]{2,0,1:T(8,128)S(1)}, u32[]{:S(2)}) copy-start(f32[64,1,256]{2,0,1:T(8,128)S(1)} %get-tuple-element.139) | copy-start | bytes 196612
  50.5 10.5 %copy-start.12 = (f32[64,1,256]{2,0,1:T(8,128)}, f32[64,1,256]{2,0,1:T(8,128)S(1)}, u32[]{:S(2)}) copy-start(f32[64,1,256]{2,0,1:T(8,128)S(1)} %get-tuple-element.144) | copy-start | bytes 196612
  50.5 10.5 %copy-start.13 = (f32[64,1,256]{2,0,1:T(8,128)}, f32[64,1,256]{2,0,1:T(8,128)S(1)}, u32[]{:S(2)}) copy-start(f32[64,1,256]{2,0,1:T(8,128)S(1)} %get-tuple-element.149) | copy-start | bytes 196612
  50.5 10.5 %copy-start.14 = (f32[64,1,256]{2,0,1:T(8,128)}, f32[64,1,256]{2,0,1:T(8,128)S(1)}, u32[]{:S(2)}) copy-start(f32[64,1,256]{2,0,1:T(8,128)S(1)} %get-tuple-element.154) | copy-start | bytes 196612
  50.6 14.0 %copy-start.16 = (f32[64,128]{1,0:T(8,128)S(1)}, f32[64,128]{1,0:T(8,128)}, u32[]{:S(2)}) copy-start(f32[64,128]{1,0:T(8,128)} %param.31) | copy-start | bytes 98308
  61.0 11.8 %all-to-all-start.2 = ((f32[64,12,256]{2,0,1:T(8,128)}), f32[64,12,256]{2,0,1:T(8,128)S(1)}, u32[]{:S(2)}, u32[]{:S(2)}) async-start(f32[64,12,256]{2,0,1:T(8,128)} %constant_dynamic-update-slice_fusion), calls=%async_computation.2 | async-start | bytes 1572864 | tf_op jit(solution)/shard_map/all_to_all | solution.py:119
  64.7 12.3 %copy-start.15 = (f32[64,128]{0,1:T(8,128)}, f32[64,128]{0,1:T(8,128)S(1)}, u32[]{:S(2)}) copy-start(f32[64,128]{0,1:T(8,128)S(1)} %copy.281) | copy-start | bytes 98308
  77.0 21.3 %copy-start.9 = (f32[2,64,3,1024]{3,1,2,0:T(8,128)S(1)}, f32[2,64,3,1024]{3,1,2,0:T(8,128)}, u32[]{:S(2)}) copy-start(f32[2,64,3,1024]{3,1,2,0:T(8,128)} %param.27) | copy-start | bytes 4718596
  77.0 414.0 %all-to-all-start.3 = ((f32[64,64,384]{2,1,0:T(8,128)}), f32[64,64,384]{2,1,0:T(8,128)}, u32[]{:S(2)}, u32[]{:S(2)}) async-start(f32[64,64,384]{2,1,0:T(8,128)} %stack.9), calls=%async_computation.3 | async-start | bytes 12582912 | tf_op jit(solution)/shard_map/all_to_all | solution.py:13
  103.1 6.1 copy-start.22
  103.1 7.4 copy-start.20
  103.2 7.4 copy-start.21
  103.2 365.8 %copy-start.19 = (s32[64]{0:T(128)S(1)}, s32[64]{0:T(128)}, u32[]{:S(2)}) copy-start(s32[64]{0:T(128)} %param.30) | copy-start | bytes 772
  472.3 3.8 slice-start.1
  585.1 4.2 copy-start.8
  613.3 334.0 %all-to-all-start.6 = ((f32[64,64,384]{2,1,0:T(8,128)}), f32[64,64,384]{2,1,0:T(8,128)}, u32[]{:S(2)}, u32[]{:S(2)}) async-start(f32[64,64,384]{2,1,0:T(8,128)} %stack.11), calls=%async_computation.6 | async-start | bytes 12582912 | tf_op jit(solution)/shard_map/all_to_all | solution.py:13
  626.3 319.6 %all-reduce.20.cloned.1.call-start = ((), (), s32[]{:S(2)}) async-start(), calls=%async_computation.7 | async-start | bytes 8388608
  626.4 7.2 copy-start.18
  (7 other events, 21.2 us)
Sparse Core Ops, SparseCore 0:
  638.4 307.4 all-reduce.19
